TPU v7x, 256 devices: a whole 4x4x8 slice. The times are simulated.
256 devices in a mesh: space: 16 (over x_hi, z), chan: 8 (over y, core), dp: 2 (over x_lo).
Axes of the slice: x: 4 (x_hi: 2, x_lo: 2; x = x_hi * 2 + x_lo), y: 4, z: 8, core: 2. Of those that a mesh axis runs over, the one named last changes fastest.
Arguments:
- inputs: bfloat16 [2, 32, 8, 128, 512], P('dp', 'space', None, 'chan'), may hold values from -6 to 6
- cotangent: bfloat16 [2, 32, 8, 128, 512], P('dp', 'space', None, 'chan'), may hold values from -6 to 6
- weight: bfloat16 [27, 128, 128], P(None, 'chan'), may hold values from -0.109375 to 0.109375
Outputs:
- input_grad: bfloat16 [2, 32, 8, 128, 512], P('dp', 'space', None, 'chan')
- weight_grad: float32 [27, 128, 128], P(None, 'chan')
All inputs are finite; a program needn't handle non-finite values.
Results may differ from a plain program's by a relative error of at most 0.001.
Values may be sent and summed in bfloat16 or wider, within the bound.
No kernel may reach another device: no remote copies, remote signals or barrier semaphores. Data moves between devices by JAX's collectives and lax.ppermute only.
A program may use at most 64 MiB of HBM per device.

v0:
```python
import math

import jax
import jax.numpy as jnp
from jax import lax
from jax.sharding import PartitionSpec as P


def from_behind(value, axis, steps):
    count = lax.axis_size(axis)
    initial, last = (max(0, -steps), min(count, count - steps))
    return lax.ppermute(value, axis, [(source, source + steps) for source in range(initial, last)])


def group_sum(value, axes, masks):
    count = lax.axis_size(axes)
    index = lax.axis_index(axes)
    members = 1 << len(masks)
    place = sum(((index & mask) != 0).astype(jnp.int32) << bit for bit, mask in enumerate(masks))
    received = [value]
    for member in range(1, members):
        flip = 0
        for bit, mask in enumerate(masks):
            if member >> bit & 1:
                flip ^= mask
        received.append(lax.ppermute(value, axes, [(i, i ^ flip) for i in range(count)]))
    ordered = []
    for member in range(members):
        choice = received[0]
        for other in range(1, members):
            choice = jnp.where((place ^ member) == other, received[other], choice)
        ordered.append(choice)
    while len(ordered) > 1:
        ordered = [ordered[k] + ordered[k + 1] for k in range(0, len(ordered), 2)]
    return ordered[0]


def flip_of(member, masks):
    flip = 0
    for bit, mask in enumerate(masks):
        if member >> bit & 1:
            flip ^= mask
    return flip


def pick(choices, selector):
    choice = choices[0]
    for other in range(1, len(choices)):
        choice = jnp.where(selector == other, choices[other], choice)
    return choice


def group_reduce(value):
    axes = ("space", "dp")
    masks = (1, 2)
    count = lax.axis_size(axes)
    index = lax.axis_index(axes)
    members = 1 << len(masks)
    place = sum(((index & mask) != 0).astype(jnp.int32) << bit for bit, mask in enumerate(masks))
    chunks = value.reshape((members, -1) + value.shape[1:])
    received = [chunks[0]]
    for member in range(1, members):
        pairs = [(i, i ^ flip_of(member, masks)) for i in range(count)]
        send = lax.dynamic_index_in_dim(chunks, place ^ member, axis=0, keepdims=False)
        received.append(lax.ppermute(send, axes, pairs))
    own = lax.dynamic_index_in_dim(chunks, place, axis=0, keepdims=False)
    received[0] = own
    ordered = [pick(received, place ^ member) for member in range(members)]
    while len(ordered) > 1:
        ordered = [ordered[k] + ordered[k + 1] for k in range(0, len(ordered), 2)]
    part = group_sum(ordered[0], axes, (4, 16))
    part = group_sum(part, axes, (8,))
    pieces = [part] + [
        lax.ppermute(part, axes, [(i, i ^ flip_of(member, masks)) for i in range(count)])
        for member in range(1, members)
    ]
    whole = [pick(pieces, place ^ member) for member in range(members)]
    return jnp.concatenate(whole, axis=0)


def gather_channels(block, axis):
    count = lax.axis_size(axis)
    own = [block] + [
        lax.ppermute(block, axis, [(i, (i + 2 * step) % count) for i in range(count)])
        for step in range(1, count // 2)
    ]
    own = jnp.stack(own)
    partner = lax.ppermute(own, axis, [(i, i ^ 1) for i in range(count)])
    index = lax.axis_index(axis)
    sources = jnp.stack(
        [(index - 2 * step) % count for step in range(count // 2)]
        + [((index ^ 1) - 2 * step) % count for step in range(count // 2)]
    )
    blocks = jnp.concatenate([own, partner], axis=0)
    return blocks, sources


def shift_cells(block, step_z, step_y):
    zero = jnp.zeros((), block.dtype)
    config = ((0, 0, 0), (0, 0, 0), (step_z, -step_z, 0), (0, 0, 0), (step_y, -step_y, 0))
    return lax.pad(block, zero, config)


def section(inputs, cotangent, weight):
    samples, planes, depth, channels, width = inputs.shape
    outputs = weight.shape[2]
    inputs_ext = jnp.concatenate(
        [from_behind(inputs[:, -1:], "space", 1), inputs, from_behind(inputs[:, :1], "space", -1)],
        axis=1,
    )
    blocks, sources = gather_channels(cotangent, "chan")
    count = blocks.shape[0]
    gathered = jnp.zeros(blocks.shape[1:4] + (count * channels,) + blocks.shape[5:], blocks.dtype)
    for place in range(count):
        gathered = lax.dynamic_update_slice_in_dim(gathered, blocks[place], sources[place] * channels, axis=3)
    contrib = {}
    for step_x in (-1, 0, 1):
        first = 9 * (step_x + 1)
        total = None
        for step_y in (-1, 0, 1):
            kernel = weight[first + step_y + 1 : first + 9 : 3].reshape(3 * channels, outputs)
            product = jnp.einsum(
                "bxzcy,kc->bxzky", gathered, kernel, preferred_element_type=jnp.float32
            )
            for place, step_z in enumerate((-1, 0, 1)):
                part = shift_cells(product[:, :, :, place * channels : (place + 1) * channels], step_z, step_y)
                total = part if total is None else total + part
        contrib[step_x] = total
    contrib, gathered = lax.optimization_barrier((contrib, gathered))
    stacked = jnp.concatenate(
        [shift_cells(inputs_ext, -step_z, -step_y) for step_z in (-1, 0, 1) for step_y in (-1, 0, 1)],
        axis=3,
    )
    groups = []
    for step_x in (-1, 0, 1):
        source = stacked[:, 1 + step_x : 1 + step_x + planes]
        groups.append(
            jnp.einsum("bxzky,bxzcy->kc", source, gathered, preferred_element_type=jnp.float32)
        )
    local_grad = jnp.concatenate(groups, axis=0).reshape(27, channels, outputs)
    count = samples * lax.axis_size("dp") * planes * lax.axis_size("space") * depth * width
    scale = 1.0 / math.sqrt(count)
    weight_grad = group_reduce(local_grad.reshape(-1, outputs)).reshape(local_grad.shape) * scale

    from_prev = from_behind(contrib[1][:, -1:], "space", 1)
    from_next = from_behind(contrib[-1][:, :1], "space", -1)
    accum = (
        contrib[0]
        + jnp.concatenate([from_prev, contrib[1][:, : planes - 1]], axis=1)
        + jnp.concatenate([contrib[-1][:, 1:], from_next], axis=1)
    )
    input_grad = accum.astype(jnp.bfloat16)
    return (input_grad, weight_grad)


def solution(mesh):
    placed = (
        P("dp", "space", None, "chan", None),
        P("dp", "space", None, "chan", None),
        P(None, "chan", None),
    )
    return jax.shard_map(
        section,
        mesh=mesh,
        in_specs=placed,
        out_specs=(P("dp", "space", None, "chan", None), P(None, "chan", None)),
        check_vma=False,
    )
```

profile of v0, /device:TPU:4, one launch (start us, length us, event | category | flops | bytes accessed | tf_op | source)
XLA Modules:
  0.0 75.3 jit_solution(10507863380026445077)
XLA Ops:
  0.6 1.7 %collective-permute-start = (bf16[1,2,8,16,512]{4,3,2,1,0:T(8,128)(2,1)}, bf16[1,2,8,16,512]{4,3,2,1,0:T(8,128)(2,1)S(1)}, u32[]{:S(2)}, u32[]{:S(2)}) collective-permute-start(bf16[1,2,8,16,512]{4,3,2,1,0:T(8,128)(2,1)} %param.4), channel_id=1, source_target_pairs={{0,4},{2,6},{4,8},{6,10},{8,12},{10,14},{12,0},{14,2},{1,5},{3,7},... | collective-permute-start | bytes 786440 | tf_op jit(solution)/shard_map/ppermute | solution.py:84
  2.3 2.9 %collective-permute-start.1 = (bf16[1,2,8,16,512]{4,3,2,1,0:T(8,128)(2,1)}, bf16[1,2,8,16,512]{4,3,2,1,0:T(8,128)(2,1)S(1)}, u32[]{:S(2)}, u32[]{:S(2)}) collective-permute-start(bf16[1,2,8,16,512]{4,3,2,1,0:T(8,128)(2,1)} %param.4), channel_id=1, source_target_pairs={{0,8},{2,10},{4,12},{6,14},{8,0},{10,2},{12,4},{14,6},{1,9},{3,11}... | collective-permute-start | bytes 786440 | tf_op jit(solution)/shard_map/ppermute | solution.py:84
  5.2 1.3 %collective-permute-start.2 = (bf16[1,2,8,16,512]{4,3,2,1,0:T(8,128)(2,1)}, bf16[1,2,8,16,512]{4,3,2,1,0:T(8,128)(2,1)S(1)}, u32[]{:S(2)}, u32[]{:S(2)}) collective-permute-start(bf16[1,2,8,16,512]{4,3,2,1,0:T(8,128)(2,1)} %param.4), channel_id=1, source_target_pairs={{0,12},{2,14},{4,0},{6,2},{8,4},{10,6},{12,8},{14,10},{1,13},{3,15... | collective-permute-start | bytes 786440 | tf_op jit(solution)/shard_map/ppermute | solution.py:84
  6.6 1.0 %fusion.120 = (bf16[1,1,8,16,512]{4,3,2,1,0:T(8,128)(2,1)S(1)}, bf16[1,1,8,16,512]{4,3,2,1,0:T(8,128)(2,1)S(1)}) fusion(bf16[1,2,8,16,512]{4,3,2,1,0:T(8,128)(2,1)} %param.3), kind=kLoop, calls=%fused_computation.162 | loop fusion | bytes 524288 | tf_op jit(solution)/shard_map/slice | solution.py:108
  7.5 3.8 %collective-permute-start.6 = (bf16[1,1,8,16,512]{4,3,2,1,0:T(8,128)(2,1)S(1)}, bf16[1,1,8,16,512]{4,3,2,1,0:T(8,128)(2,1)S(1)}, u32[]{:S(2)}, u32[]{:S(2)}) collective-permute-start(bf16[1,1,8,16,512]{4,3,2,1,0:T(8,128)(2,1)S(1)} %get-tuple-element.39), channel_id=1, source_target_pairs={{0,16},{16,32},{32,48},{48,64},{64,80},{80,96},{96,112},{112,128},... | collective-permute-start | bytes 393224 | tf_op jit(solution)/shard_map/ppermute | solution.py:12
  11.4 5.8 %collective-permute-start.7 = (bf16[1,1,8,16,512]{4,3,2,1,0:T(8,128)(2,1)S(1)}, bf16[1,1,8,16,512]{4,3,2,1,0:T(8,128)(2,1)S(1)}, u32[]{:S(2)}, u32[]{:S(2)}) collective-permute-start(bf16[1,1,8,16,512]{4,3,2,1,0:T(8,128)(2,1)S(1)} %get-tuple-element.38), channel_id=1, source_target_pairs={{16,0},{32,16},{48,32},{64,48},{80,64},{96,80},{112,96},{128,112},... | collective-permute-start | bytes 393224 | tf_op jit(solution)/shard_map/ppermute | solution.py:12
  17.2 0.9 %fusion.121 = (bf16[3,16,128]{2,1,0:T(8,128)(2,1)S(1)}, bf16[3,16,128]{2,1,0:T(8,128)(2,1)S(1)}, bf16[3,16,128]{2,1,0:T(8,128)(2,1)S(1)}, bf16[3,16,128]{2,1,0:T...) fusion(bf16[27,16,128]{2,1,0:T(8,128)(2,1)} %param.5), kind=kLoop, calls=%fused_computation.163 | loop fusion | bytes 221184 | tf_op jit(solution)/shard_map/slice | solution.py:121
  18.5 1.1 %collective-permute-done.7 = bf16[1,1,8,16,512]{4,3,2,1,0:T(8,128)(2,1)S(1)} collective-permute-done((bf16[1,1,8,16,512]{4,3,2,1,0:T(8,128)(2,1)S(1)}, bf16[1,1,8,16,512]{4,3,2,1,0:T(8,128)(2,1)S(1)}, u32[]{:S(2)}, u32[]{:S(2)}) %collective-permute-start.7) | collective-permute-done | bytes 131104 | tf_op jit(solution)/shard_map/ppermute | solution.py:12
  22.0 1.7 %collective-permute-done.3 = bf16[4,1,2,8,16,512]{5,4,3,2,1,0:T(8,128)(2,1)S(1)} collective-permute-done((bf16[4,1,2,8,16,512]{5,4,3,2,1,0:T(8,128)(2,1)S(1)}, bf16[4,1,2,8,16,512]{5,4,3,2,1,0:T(8,128)(2,1)S(1)}, u32[]{:S(2)}, u32[]{:S(2)}) %collective-permute-start.3) | collective-permute-done | bytes 1048608 | tf_op jit(solution)/shard_map/ppermute | solution.py:88
  29.7 0.8 %fusion.67 = f32[1,2,8,16,512]{4,3,2,1,0:T(8,128)S(1)} fusion(f32[1,2,8,16,512]{4,3,2,1,0:T(8,128)S(1)} %get-tuple-element.33, f32[1,2,8,16,512]{4,3,2,1,0:T(8,128)S(1)} %get-tuple-element.32, f32[1,2,8,16,512]{4,3,2,1,0:T(8,128)S(1)} %get-tuple-element.57, f32[1,2,8,16,512]{4,3,2,1,0:T(8,128)S(1)} %get-tuple-element.27, ...), kind=kLoop, calls=%fused_computation.79 | loop fusion | flops 1048576 | bytes 5242880 | tf_op jit(solution)/shard_map/add | solution.py:127
  30.5 0.8 %fusion.73 = f32[1,2,8,16,512]{4,3,2,1,0:T(8,128)S(1)} fusion(f32[1,2,8,16,512]{4,3,2,1,0:T(8,128)S(1)} %get-tuple-element.25, f32[1,2,8,16,512]{4,3,2,1,0:T(8,128)S(1)} %get-tuple-element.24, f32[1,2,8,16,512]{4,3,2,1,0:T(8,128)S(1)} %get-tuple-element.60, f32[1,2,8,16,512]{4,3,2,1,0:T(8,128)S(1)} %get-tuple-element.19, ...), kind=kLoop, calls=%fused_computation.85 | loop fusion | flops 1048576 | bytes 5242880 | tf_op jit(solution)/shard_map/add | solution.py:127
  31.3 0.8 %fusion.79 = f32[1,2,8,16,512]{4,3,2,1,0:T(8,128)S(1)} fusion(f32[1,2,8,16,512]{4,3,2,1,0:T(8,128)S(1)} %get-tuple-element.17, f32[1,2,8,16,512]{4,3,2,1,0:T(8,128)S(1)} %get-tuple-element.16, f32[1,2,8,16,512]{4,3,2,1,0:T(8,128)S(1)} %get-tuple-element.63, f32[1,2,8,16,512]{4,3,2,1,0:T(8,128)S(1)} %get-tuple-element.11, ...), kind=kLoop, calls=%fused_computation.91 | loop fusion | flops 1048576 | bytes 5242880 | tf_op jit(solution)/shard_map/add | solution.py:127
  32.1 0.8 %fusion.57 = f32[144,128]{1,0:T(8,128)S(1)} fusion(bf16[1,2,8,128,512]{4,3,2,1,0:T(8,128)(2,1)S(1)} %fusion.94, bf16[1,4,8,144,512]{4,3,2,1,0:T(8,128)(2,1)S(1)} %fusion.91), kind=kOutput, calls=%fused_computation.38 | convolution fusion | flops 301989888 | bytes 4530176 | tf_op jit(solution)/shard_map/bxzky,bxzcy->kc/dot_general | solution.py:138
  33.7 0.8 %fusion.51 = f32[144,128]{1,0:T(8,128)S(1)} fusion(bf16[1,2,8,128,512]{4,3,2,1,0:T(8,128)(2,1)S(1)} %fusion.94, bf16[1,4,8,144,512]{4,3,2,1,0:T(8,128)(2,1)S(1)} %fusion.91), kind=kOutput, calls=%fused_computation.36 | convolution fusion | flops 301989888 | bytes 4530176 | tf_op jit(solution)/shard_map/bxzky,bxzcy->kc/dot_general | solution.py:138
  34.5 1.2 %collective-permute-start.8 = (f32[108,128]{1,0:T(8,128)S(1)}, f32[108,128]{1,0:T(8,128)S(1)}, u32[]{:S(2)}, u32[]{:S(2)}) collective-permute-start(f32[108,128]{1,0:T(8,128)S(1)} %get-tuple-element.46), channel_id=1, source_target_pairs={{0,17},{1,16},{16,1},{17,0},{32,49},{33,48},{48,33},{49,32},{64,81... | collective-permute-start | bytes 165896 | tf_op jit(solution)/shard_map/ppermute | solution.py:65
  35.7 2.5 %collective-permute-start.9 = (f32[108,128]{1,0:T(8,128)S(1)}, f32[108,128]{1,0:T(8,128)S(1)}, u32[]{:S(2)}, u32[]{:S(2)}) collective-permute-start(f32[108,128]{1,0:T(8,128)S(1)} %get-tuple-element.45), channel_id=1, source_target_pairs={{0,16},{1,17},{16,0},{17,1},{32,48},{33,49},{48,32},{49,33},{64,80... | collective-permute-start | bytes 165896 | tf_op jit(solution)/shard_map/ppermute | solution.py:65
  38.2 2.0 %collective-permute-done.8 = f32[108,128]{1,0:T(8,128)S(1)} collective-permute-done((f32[108,128]{1,0:T(8,128)S(1)}, f32[108,128]{1,0:T(8,128)S(1)}, u32[]{:S(2)}, u32[]{:S(2)}) %collective-permute-start.8) | collective-permute-done | bytes 55328 | tf_op jit(solution)/shard_map/ppermute | solution.py:65
  40.2 1.1 %collective-permute-done.9 = f32[108,128]{1,0:T(8,128)S(1)} collective-permute-done((f32[108,128]{1,0:T(8,128)S(1)}, f32[108,128]{1,0:T(8,128)S(1)}, u32[]{:S(2)}, u32[]{:S(2)}) %collective-permute-start.9) | collective-permute-done | bytes 55328 | tf_op jit(solution)/shard_map/ppermute | solution.py:65
  41.3 1.0 %collective-permute-done.10 = f32[108,128]{1,0:T(8,128)S(1)} collective-permute-done((f32[108,128]{1,0:T(8,128)S(1)}, f32[108,128]{1,0:T(8,128)S(1)}, u32[]{:S(2)}, u32[]{:S(2)}) %collective-permute-start.10) | collective-permute-done | bytes 55328 | tf_op jit(solution)/shard_map/ppermute | solution.py:65
  42.4 3.6 %collective-permute-start.11 = (f32[108,128]{1,0:T(8,128)S(1)}, f32[108,128]{1,0:T(8,128)S(1)}, u32[]{:S(2)}, u32[]{:S(2)}) collective-permute-start(f32[108,128]{1,0:T(8,128)S(1)} %fusion.101), channel_id=1, source_target_pairs={{0,160},{1,161},{16,176},{17,177},{32,128},{33,129},{48,144},{49,1... | collective-permute-start | bytes 165896 | tf_op jit(solution)/shard_map/ppermute | solution.py:26
  45.9 2.7 %collective-permute-start.12 = (f32[108,128]{1,0:T(8,128)S(1)}, f32[108,128]{1,0:T(8,128)S(1)}, u32[]{:S(2)}, u32[]{:S(2)}) collective-permute-start(f32[108,128]{1,0:T(8,128)S(1)} %fusion.101), channel_id=1, source_target_pairs={{0,128},{1,129},{16,144},{17,145},{32,160},{33,161},{48,176},{49,1... | collective-permute-start | bytes 165896 | tf_op jit(solution)/shard_map/ppermute | solution.py:26
  48.7 1.5 %collective-permute-done.11 = f32[108,128]{1,0:T(8,128)S(1)} collective-permute-done((f32[108,128]{1,0:T(8,128)S(1)}, f32[108,128]{1,0:T(8,128)S(1)}, u32[]{:S(2)}, u32[]{:S(2)}) %collective-permute-start.11) | collective-permute-done | bytes 55328 | tf_op jit(solution)/shard_map/ppermute | solution.py:26
  50.2 1.5 %collective-permute-done.12 = f32[108,128]{1,0:T(8,128)S(1)} collective-permute-done((f32[108,128]{1,0:T(8,128)S(1)}, f32[108,128]{1,0:T(8,128)S(1)}, u32[]{:S(2)}, u32[]{:S(2)}) %collective-permute-start.12) | collective-permute-done | bytes 55328 | tf_op jit(solution)/shard_map/ppermute | solution.py:26
  51.6 2.1 %collective-permute-done.13 = f32[108,128]{1,0:T(8,128)S(1)} collective-permute-done((f32[108,128]{1,0:T(8,128)S(1)}, f32[108,128]{1,0:T(8,128)S(1)}, u32[]{:S(2)}, u32[]{:S(2)}) %collective-permute-start.13) | collective-permute-done | bytes 55328 | tf_op jit(solution)/shard_map/ppermute | solution.py:26
  53.8 2.9 %collective-permute-start.14 = (f32[108,128]{1,0:T(8,128)S(1)}, f32[108,128]{1,0:T(8,128)S(1)}, u32[]{:S(2)}, u32[]{:S(2)}) collective-permute-start(f32[108,128]{1,0:T(8,128)S(1)} %add_add_fusion), channel_id=1, source_target_pairs={{0,64},{1,65},{16,80},{17,81},{32,96},{33,97},{48,112},{49,113},{6... | collective-permute-start | bytes 165896 | tf_op jit(solution)/shard_map/ppermute | solution.py:26
  56.7 2.8 %collective-permute-start.4 = (f32[1,1,8,16,512]{4,3,2,1,0:T(8,128)S(1)}, f32[1,1,8,16,512]{4,3,2,1,0:T(8,128)S(1)}, u32[]{:S(2)}, u32[]{:S(2)}) collective-permute-start(f32[1,1,8,16,512]{4,3,2,1,0:T(8,128)S(1)} %get-tuple-element.36), channel_id=1, source_target_pairs={{0,16},{16,32},{32,48},{48,64},{64,80},{80,96},{96,112},{112,128},... | collective-permute-start | bytes 786440 | tf_op jit(solution)/shard_map/ppermute | solution.py:12
  59.5 2.7 %collective-permute-done.14 = f32[108,128]{1,0:T(8,128)S(1)} collective-permute-done((f32[108,128]{1,0:T(8,128)S(1)}, f32[108,128]{1,0:T(8,128)S(1)}, u32[]{:S(2)}, u32[]{:S(2)}) %collective-permute-start.14) | collective-permute-done | bytes 55328 | tf_op jit(solution)/shard_map/ppermute | solution.py:26
  62.2 3.1 %collective-permute-start.15 = (f32[108,128]{1,0:T(8,128)S(1)}, f32[108,128]{1,0:T(8,128)S(1)}, u32[]{:S(2)}, u32[]{:S(2)}) collective-permute-start(f32[108,128]{1,0:T(8,128)S(1)} %select_add_fusion), channel_id=1, source_target_pairs={{0,17},{1,16},{16,1},{17,0},{32,49},{33,48},{48,33},{49,32},{64,81... | collective-permute-start | bytes 165896 | tf_op jit(solution)/shard_map/ppermute | solution.py:74
  65.3 0.9 %collective-permute-start.17 = (f32[108,128]{1,0:T(8,128)S(1)}, f32[108,128]{1,0:T(8,128)S(1)}, u32[]{:S(2)}, u32[]{:S(2)}) collective-permute-start(f32[108,128]{1,0:T(8,128)S(1)} %select_add_fusion), channel_id=1, source_target_pairs={{0,1},{1,0},{16,17},{17,16},{32,33},{33,32},{48,49},{49,48},{64,65... | collective-permute-start | bytes 165896 | tf_op jit(solution)/shard_map/ppermute | solution.py:74
  66.2 4.1 %collective-permute-start.5 = (f32[1,1,8,16,512]{4,3,2,1,0:T(8,128)S(1)}, f32[1,1,8,16,512]{4,3,2,1,0:T(8,128)S(1)}, u32[]{:S(2)}, u32[]{:S(2)}) collective-permute-start(f32[1,1,8,16,512]{4,3,2,1,0:T(8,128)S(1)} %get-tuple-element.35), channel_id=1, source_target_pairs={{16,0},{32,16},{48,32},{64,48},{80,64},{96,80},{112,96},{128,112},... | collective-permute-start | bytes 786440 | tf_op jit(solution)/shard_map/ppermute | solution.py:12
  71.1 3.4 %collective-permute-done.5 = f32[1,1,8,16,512]{4,3,2,1,0:T(8,128)S(1)} collective-permute-done((f32[1,1,8,16,512]{4,3,2,1,0:T(8,128)S(1)}, f32[1,1,8,16,512]{4,3,2,1,0:T(8,128)S(1)}, u32[]{:S(2)}, u32[]{:S(2)}) %collective-permute-start.5) | collective-permute-done | bytes 262176 | tf_op jit(solution)/shard_map/ppermute | solution.py:12
  74.5 0.8 %fusion.93 = bf16[1,2,8,16,512]{4,3,2,1,0:T(8,128)(2,1)} fusion(f32[1,2,8,16,512]{4,3,2,1,0:T(8,128)S(1)} %fusion.73, f32[1,1,8,16,512]{4,3,2,1,0:T(8,128)S(1)} %get-tuple-element.37, f32[1,1,8,16,512]{4,3,2,1,0:T(8,128)S(1)} %collective-permute-done.4, f32[1,1,8,16,512]{4,3,2,1,0:T(8,128)S(1)} %collective-permute-done.5, ...), kind=kLoop, calls=%fused_computation.106 | loop fusion | flops 655360 | bytes 1835008 | tf_op jit(solution)/shard_map/convert_element_type | solution.py:152
  (66 shorter events, 10.1 us)
Async XLA Ops:
  0.6 17.8 %copy-start.1 = (bf16[1,2,8,16,512]{4,3,2,1,0:T(8,128)(2,1)S(1)}, bf16[1,2,8,16,512]{4,3,2,1,0:T(8,128)(2,1)}, u32[]{:S(2)}) copy-start(bf16[1,2,8,16,512]{4,3,2,1,0:T(8,128)(2,1)} %param.4) | copy-start | bytes 786436
  0.6 17.9 %copy-start = (bf16[1,2,8,16,512]{4,3,2,1,0:T(8,128)(2,1)S(1)}, bf16[1,2,8,16,512]{4,3,2,1,0:T(8,128)(2,1)}, u32[]{:S(2)}) copy-start(bf16[1,2,8,16,512]{4,3,2,1,0:T(8,128)(2,1)} %param.3) | copy-start | bytes 786436
  0.6 19.9 %collective-permute-start = (bf16[1,2,8,16,512]{4,3,2,1,0:T(8,128)(2,1)}, bf16[1,2,8,16,512]{4,3,2,1,0:T(8,128)(2,1)S(1)}, u32[]{:S(2)}, u32[]{:S(2)}) collective-permute-start(bf16[1,2,8,16,512]{4,3,2,1,0:T(8,128)(2,1)} %param.4), channel_id=1, source_target_pairs={{0,4},{2,6},{4,8},{6,10},{8,12},{10,14},{12,0},{14,2},{1,5},{3,7},... | collective-permute-start | bytes 786440 | tf_op jit(solution)/shard_map/ppermute | solution.py:84
  2.3 18.3 %collective-permute-start.1 = (bf16[1,2,8,16,512]{4,3,2,1,0:T(8,128)(2,1)}, bf16[1,2,8,16,512]{4,3,2,1,0:T(8,128)(2,1)S(1)}, u32[]{:S(2)}, u32[]{:S(2)}) collective-permute-start(bf16[1,2,8,16,512]{4,3,2,1,0:T(8,128)(2,1)} %param.4), channel_id=1, source_target_pairs={{0,8},{2,10},{4,12},{6,14},{8,0},{10,2},{12,4},{14,6},{1,9},{3,11}... | collective-permute-start | bytes 786440 | tf_op jit(solution)/shard_map/ppermute | solution.py:84
  5.2 15.4 %collective-permute-start.2 = (bf16[1,2,8,16,512]{4,3,2,1,0:T(8,128)(2,1)}, bf16[1,2,8,16,512]{4,3,2,1,0:T(8,128)(2,1)S(1)}, u32[]{:S(2)}, u32[]{:S(2)}) collective-permute-start(bf16[1,2,8,16,512]{4,3,2,1,0:T(8,128)(2,1)} %param.4), channel_id=1, source_target_pairs={{0,12},{2,14},{4,0},{6,2},{8,4},{10,6},{12,8},{14,10},{1,13},{3,15... | collective-permute-start | bytes 786440 | tf_op jit(solution)/shard_map/ppermute | solution.py:84
  7.5 10.9 %collective-permute-start.6 = (bf16[1,1,8,16,512]{4,3,2,1,0:T(8,128)(2,1)S(1)}, bf16[1,1,8,16,512]{4,3,2,1,0:T(8,128)(2,1)S(1)}, u32[]{:S(2)}, u32[]{:S(2)}) collective-permute-start(bf16[1,1,8,16,512]{4,3,2,1,0:T(8,128)(2,1)S(1)} %get-tuple-element.39), channel_id=1, source_target_pairs={{0,16},{16,32},{32,48},{48,64},{64,80},{80,96},{96,112},{112,128},... | collective-permute-start | bytes 393224 | tf_op jit(solution)/shard_map/ppermute | solution.py:12
  11.4 8.3 %collective-permute-start.7 = (bf16[1,1,8,16,512]{4,3,2,1,0:T(8,128)(2,1)S(1)}, bf16[1,1,8,16,512]{4,3,2,1,0:T(8,128)(2,1)S(1)}, u32[]{:S(2)}, u32[]{:S(2)}) collective-permute-start(bf16[1,1,8,16,512]{4,3,2,1,0:T(8,128)(2,1)S(1)} %get-tuple-element.38), channel_id=1, source_target_pairs={{16,0},{32,16},{48,32},{64,48},{80,64},{96,80},{112,96},{128,112},... | collective-permute-start | bytes 393224 | tf_op jit(solution)/shard_map/ppermute | solution.py:12
  20.7 2.9 %collective-permute-start.3 = (bf16[4,1,2,8,16,512]{5,4,3,2,1,0:T(8,128)(2,1)S(1)}, bf16[4,1,2,8,16,512]{5,4,3,2,1,0:T(8,128)(2,1)S(1)}, u32[]{:S(2)}, u32[]{:S(2)}) collective-permute-start(bf16[4,1,2,8,16,512]{5,4,3,2,1,0:T(8,128)(2,1)S(1)} %pad_maximum_fusion), channel_id=1, source_target_pairs={{0,2},{2,0},{4,6},{6,4},{8,10},{10,8},{12,14},{14,12},{1,3},{3,1},... | collective-permute-start | bytes 3145736 | tf_op jit(solution)/shard_map/ppermute | solution.py:88
  34.5 5.7 %collective-permute-start.8 = (f32[108,128]{1,0:T(8,128)S(1)}, f32[108,128]{1,0:T(8,128)S(1)}, u32[]{:S(2)}, u32[]{:S(2)}) collective-permute-start(f32[108,128]{1,0:T(8,128)S(1)} %get-tuple-element.46), channel_id=1, source_target_pairs={{0,17},{1,16},{16,1},{17,0},{32,49},{33,48},{48,33},{49,32},{64,81... | collective-permute-start | bytes 165896 | tf_op jit(solution)/shard_map/ppermute | solution.py:65
  35.7 5.6 %collective-permute-start.9 = (f32[108,128]{1,0:T(8,128)S(1)}, f32[108,128]{1,0:T(8,128)S(1)}, u32[]{:S(2)}, u32[]{:S(2)}) collective-permute-start(f32[108,128]{1,0:T(8,128)S(1)} %get-tuple-element.45), channel_id=1, source_target_pairs={{0,16},{1,17},{16,0},{17,1},{32,48},{33,49},{48,32},{49,33},{64,80... | collective-permute-start | bytes 165896 | tf_op jit(solution)/shard_map/ppermute | solution.py:65
  38.2 4.2 %collective-permute-start.10 = (f32[108,128]{1,0:T(8,128)S(1)}, f32[108,128]{1,0:T(8,128)S(1)}, u32[]{:S(2)}, u32[]{:S(2)}) collective-permute-start(f32[108,128]{1,0:T(8,128)S(1)} %get-tuple-element.44), channel_id=1, source_target_pairs={{0,1},{1,0},{16,17},{17,16},{32,33},{33,32},{48,49},{49,48},{64,65... | collective-permute-start | bytes 165896 | tf_op jit(solution)/shard_map/ppermute | solution.py:65
  42.4 7.8 %collective-permute-start.11 = (f32[108,128]{1,0:T(8,128)S(1)}, f32[108,128]{1,0:T(8,128)S(1)}, u32[]{:S(2)}, u32[]{:S(2)}) collective-permute-start(f32[108,128]{1,0:T(8,128)S(1)} %fusion.101), channel_id=1, source_target_pairs={{0,160},{1,161},{16,176},{17,177},{32,128},{33,129},{48,144},{49,1... | collective-permute-start | bytes 165896 | tf_op jit(solution)/shard_map/ppermute | solution.py:26
  45.9 5.7 %collective-permute-start.12 = (f32[108,128]{1,0:T(8,128)S(1)}, f32[108,128]{1,0:T(8,128)S(1)}, u32[]{:S(2)}, u32[]{:S(2)}) collective-permute-start(f32[108,128]{1,0:T(8,128)S(1)} %fusion.101), channel_id=1, source_target_pairs={{0,128},{1,129},{16,144},{17,145},{32,160},{33,161},{48,176},{49,1... | collective-permute-start | bytes 165896 | tf_op jit(solution)/shard_map/ppermute | solution.py:26
  48.7 5.1 %collective-permute-start.13 = (f32[108,128]{1,0:T(8,128)S(1)}, f32[108,128]{1,0:T(8,128)S(1)}, u32[]{:S(2)}, u32[]{:S(2)}) collective-permute-start(f32[108,128]{1,0:T(8,128)S(1)} %fusion.101), channel_id=1, source_target_pairs={{0,32},{1,33},{16,48},{17,49},{32,0},{33,1},{48,16},{49,17},{64,96... | collective-permute-start | bytes 165896 | tf_op jit(solution)/shard_map/ppermute | solution.py:26
  53.8 8.4 %collective-permute-start.14 = (f32[108,128]{1,0:T(8,128)S(1)}, f32[108,128]{1,0:T(8,128)S(1)}, u32[]{:S(2)}, u32[]{:S(2)}) collective-permute-start(f32[108,128]{1,0:T(8,128)S(1)} %add_add_fusion), channel_id=1, source_target_pairs={{0,64},{1,65},{16,80},{17,81},{32,96},{33,97},{48,112},{49,113},{6... | collective-permute-start | bytes 165896 | tf_op jit(solution)/shard_map/ppermute | solution.py:26
  56.7 14.4 %collective-permute-start.4 = (f32[1,1,8,16,512]{4,3,2,1,0:T(8,128)S(1)}, f32[1,1,8,16,512]{4,3,2,1,0:T(8,128)S(1)}, u32[]{:S(2)}, u32[]{:S(2)}) collective-permute-start(f32[1,1,8,16,512]{4,3,2,1,0:T(8,128)S(1)} %get-tuple-element.36), channel_id=1, source_target_pairs={{0,16},{16,32},{32,48},{48,64},{64,80},{80,96},{96,112},{112,128},... | collective-permute-start | bytes 786440 | tf_op jit(solution)/shard_map/ppermute | solution.py:12
  62.2 8.1 %collective-permute-start.15 = (f32[108,128]{1,0:T(8,128)S(1)}, f32[108,128]{1,0:T(8,128)S(1)}, u32[]{:S(2)}, u32[]{:S(2)}) collective-permute-start(f32[108,128]{1,0:T(8,128)S(1)} %select_add_fusion), channel_id=1, source_target_pairs={{0,17},{1,16},{16,1},{17,0},{32,49},{33,48},{48,33},{49,32},{64,81... | collective-permute-start | bytes 165896 | tf_op jit(solution)/shard_map/ppermute | solution.py:74
  65.3 5.0 %collective-permute-start.16 = (f32[108,128]{1,0:T(8,128)S(1)}, f32[108,128]{1,0:T(8,128)S(1)}, u32[]{:S(2)}, u32[]{:S(2)}) collective-permute-start(f32[108,128]{1,0:T(8,128)S(1)} %select_add_fusion), channel_id=1, source_target_pairs={{0,16},{1,17},{16,0},{17,1},{32,48},{33,49},{48,32},{49,33},{64,80... | collective-permute-start | bytes 165896 | tf_op jit(solution)/shard_map/ppermute | solution.py:74
  65.3 5.0 %collective-permute-start.17 = (f32[108,128]{1,0:T(8,128)S(1)}, f32[108,128]{1,0:T(8,128)S(1)}, u32[]{:S(2)}, u32[]{:S(2)}) collective-permute-start(f32[108,128]{1,0:T(8,128)S(1)} %select_add_fusion), channel_id=1, source_target_pairs={{0,1},{1,0},{16,17},{17,16},{32,33},{33,32},{48,49},{49,48},{64,65... | collective-permute-start | bytes 165896 | tf_op jit(solution)/shard_map/ppermute | solution.py:74
  66.2 8.3 %collective-permute-start.5 = (f32[1,1,8,16,512]{4,3,2,1,0:T(8,128)S(1)}, f32[1,1,8,16,512]{4,3,2,1,0:T(8,128)S(1)}, u32[]{:S(2)}, u32[]{:S(2)}) collective-permute-start(f32[1,1,8,16,512]{4,3,2,1,0:T(8,128)S(1)} %get-tuple-element.35), channel_id=1, source_target_pairs={{16,0},{32,16},{48,32},{64,48},{80,64},{96,80},{112,96},{128,112},... | collective-permute-start | bytes 786440 | tf_op jit(solution)/shard_map/ppermute | solution.py:12
where the time goes:
time: 76 us; the launch traced here: 75.3 us
  starting transfers between devices  39.4 us (52%)
  waiting for transfers between devices  18.1 us (24%)
  matrix products  6.11 us (8%)
  local copies, waits for them, and re-layouts  6.08 us (8%)
  other arithmetic  4.23 us (6%)
  between operations  1.29 us (2%)
    ppermute x4, starting transfers between devices, from_behind(): lax.ppermute(value, axis, [(source, source + steps) for source in range(i...  16.5 us
    ppermute x4, starting transfers between devices, group_sum(): lax.ppermute(value, axes, [(i, i ^ flip) for i in range(count)])  9.17 us
    ppermute x4, waiting for transfers between devices, group_sum(): lax.ppermute(value, axes, [(i, i ^ flip) for i in range(count)])  7.74 us
    ppermute x3, starting transfers between devices, gather_channels(): lax.ppermute(block, axis, [(i, (i + 2 * step) % count) for i in range(cou...  5.9 us
    ppermute x4, waiting for transfers between devices, from_behind(): lax.ppermute(value, axis, [(source, source + steps) for source in range(i...  4.54 us
    ppermute x3, waiting for transfers between devices, group_reduce(): received.append(lax.ppermute(send, axes, pairs))  4.17 us
    ppermute x3, starting transfers between devices, group_reduce(): lax.ppermute(part, axes, [(i, i ^ flip_of(member, masks)) for i in range(...  3.94 us
    dot_general x9, matrix products, section(): jnp.einsum('bxzcy,kc->bxzky', gathered, kernel, preferred_element_type=jn...  3.82 us
  transfers between devices with their start and end apart: 18, of which 10 were waited for; matrix products, arithmetic and copies ran while one was open for 6% of the time, Pallas kernels for 0%

commit v1 on v0

--- a/solution.py
+++ b/solution.py
@@ -84,8 +84,11 @@
         lax.ppermute(block, axis, [(i, (i + 2 * step) % count) for i in range(count)])
         for step in range(1, count // 2)
     ]
+    swap = [(i, i ^ 1) for i in range(count)]
+    partner = jnp.concatenate(
+        [lax.ppermute(block, axis, swap)[None], lax.ppermute(jnp.stack(own[1:]), axis, swap)], axis=0
+    )
     own = jnp.stack(own)
-    partner = lax.ppermute(own, axis, [(i, i ^ 1) for i in range(count)])
     index = lax.axis_index(axis)
     sources = jnp.stack(
         [(index - 2 * step) % count for step in range(count // 2)]

time: 76 us -> 82.3 us (1.083)
  waiting for transfers between devices: 18.1 us -> 22.9 us
  starting transfers between devices: 39.4 us -> 41.2 us
    ppermute x4, waiting for transfers between devices: 4.54 us -> 13.3 us  [from_behind(): lax.ppermute(value, axis, [(source, source + steps) for source in range(i...]
    ppermute x4, waiting for transfers between devices: 7.74 us -> 3.72 us  [group_sum(): lax.ppermute(value, axes, [(i, i ^ flip) for i in range(count)])]
    ppermute x4, starting transfers between devices: 16.5 us -> 18.4 us  [from_behind(): lax.ppermute(value, axis, [(source, source + steps) for source in range(i...]
    ppermute x1 -> x2, waiting for transfers between devices: 1.65 us -> 1.61 us  [the longest x1 1.6 us: gather_channels(): lax.ppermute(jnp.stack(own[1:]), axis, swap)]
  transfers between devices with their start and end apart: 18 -> 19, of which waited for: 10 -> 10; matrix products, arithmetic and copies ran while one was open for 6% -> 6% of each run, Pallas kernels for 0% -> 0%
where the time goes in v1:
time: 82.3 us; the launch traced here: 81.7 us
  starting transfers between devices  41.2 us (50%)
  waiting for transfers between devices  22.9 us (28%)
  matrix products  6.12 us (7%)
  local copies, waits for them, and re-layouts  6.06 us (7%)
  other arithmetic  4.19 us (5%)
  between operations  1.29 us (2%)
    ppermute x4, starting transfers between devices, from_behind(): lax.ppermute(value, axis, [(source, source + steps) for source in range(i...  18.4 us
    ppermute x4, waiting for transfers between devices, from_behind(): lax.ppermute(value, axis, [(source, source + steps) for source in range(i...  13.3 us
    ppermute x4, starting transfers between devices, group_sum(): lax.ppermute(value, axes, [(i, i ^ flip) for i in range(count)])  9.45 us
    ppermute x3, starting transfers between devices, gather_channels(): lax.ppermute(block, axis, [(i, (i + 2 * step) % count) for i in range(cou...  5.9 us
    ppermute x3, waiting for transfers between devices, group_reduce(): received.append(lax.ppermute(send, axes, pairs))  4.17 us
    dot_general x9, matrix products, section(): jnp.einsum('bxzcy,kc->bxzky', gathered, kernel, preferred_element_type=jn...  3.82 us
    ppermute x4, waiting for transfers between devices, group_sum(): lax.ppermute(value, axes, [(i, i ^ flip) for i in range(count)])  3.72 us
    ppermute x3, starting transfers between devices, group_reduce(): received.append(lax.ppermute(send, axes, pairs))  3.66 us
  transfers between devices with their start and end apart: 19, of which 10 were waited for; matrix products, arithmetic and copies ran while one was open for 6% of the time, Pallas kernels for 0%

profile of v1, /device:TPU:4, one launch (start us, length us, event | category | flops | bytes accessed | tf_op | source)
XLA Modules:
  0.0 81.7 jit_solution(8828663755544357352)
XLA Ops:
  0.6 1.7 %collective-permute-start = (bf16[1,2,8,16,512]{4,3,2,1,0:T(8,128)(2,1)}, bf16[1,2,8,16,512]{4,3,2,1,0:T(8,128)(2,1)S(1)}, u32[]{:S(2)}, u32[]{:S(2)}) collective-permute-start(bf16[1,2,8,16,512]{4,3,2,1,0:T(8,128)(2,1)} %param.4), channel_id=1, source_target_pairs={{0,4},{2,6},{4,8},{6,10},{8,12},{10,14},{12,0},{14,2},{1,5},{3,7},... | collective-permute-start | bytes 786440 | tf_op jit(solution)/shard_map/ppermute | solution.py:84
  2.3 2.9 %collective-permute-start.1 = (bf16[1,2,8,16,512]{4,3,2,1,0:T(8,128)(2,1)}, bf16[1,2,8,16,512]{4,3,2,1,0:T(8,128)(2,1)S(1)}, u32[]{:S(2)}, u32[]{:S(2)}) collective-permute-start(bf16[1,2,8,16,512]{4,3,2,1,0:T(8,128)(2,1)} %param.4), channel_id=1, source_target_pairs={{0,8},{2,10},{4,12},{6,14},{8,0},{10,2},{12,4},{14,6},{1,9},{3,11}... | collective-permute-start | bytes 786440 | tf_op jit(solution)/shard_map/ppermute | solution.py:84
  5.2 1.3 %collective-permute-start.2 = (bf16[1,2,8,16,512]{4,3,2,1,0:T(8,128)(2,1)}, bf16[1,2,8,16,512]{4,3,2,1,0:T(8,128)(2,1)S(1)}, u32[]{:S(2)}, u32[]{:S(2)}) collective-permute-start(bf16[1,2,8,16,512]{4,3,2,1,0:T(8,128)(2,1)} %param.4), channel_id=1, source_target_pairs={{0,12},{2,14},{4,0},{6,2},{8,4},{10,6},{12,8},{14,10},{1,13},{3,15... | collective-permute-start | bytes 786440 | tf_op jit(solution)/shard_map/ppermute | solution.py:84
  6.6 1.0 %fusion.119 = (bf16[1,1,8,16,512]{4,3,2,1,0:T(8,128)(2,1)S(1)}, bf16[1,1,8,16,512]{4,3,2,1,0:T(8,128)(2,1)S(1)}) fusion(bf16[1,2,8,16,512]{4,3,2,1,0:T(8,128)(2,1)} %param.3), kind=kLoop, calls=%fused_computation.161 | loop fusion | bytes 524288 | tf_op jit(solution)/shard_map/slice | solution.py:111
  7.5 3.8 %collective-permute-start.7 = (bf16[1,1,8,16,512]{4,3,2,1,0:T(8,128)(2,1)S(1)}, bf16[1,1,8,16,512]{4,3,2,1,0:T(8,128)(2,1)S(1)}, u32[]{:S(2)}, u32[]{:S(2)}) collective-permute-start(bf16[1,1,8,16,512]{4,3,2,1,0:T(8,128)(2,1)S(1)} %get-tuple-element.39), channel_id=1, source_target_pairs={{0,16},{16,32},{32,48},{48,64},{64,80},{80,96},{96,112},{112,128},... | collective-permute-start | bytes 393224 | tf_op jit(solution)/shard_map/ppermute | solution.py:12
  11.4 0.9 %fusion.120 = (bf16[3,16,128]{2,1,0:T(8,128)(2,1)S(1)}, bf16[3,16,128]{2,1,0:T(8,128)(2,1)S(1)}, bf16[3,16,128]{2,1,0:T(8,128)(2,1)S(1)}, bf16[3,16,128]{2,1,0:T...) fusion(bf16[27,16,128]{2,1,0:T(8,128)(2,1)} %param.5), kind=kLoop, calls=%fused_computation.162 | loop fusion | bytes 221184 | tf_op jit(solution)/shard_map/slice | solution.py:124
  12.7 6.7 %collective-permute-done.7 = bf16[1,1,8,16,512]{4,3,2,1,0:T(8,128)(2,1)S(1)} collective-permute-done((bf16[1,1,8,16,512]{4,3,2,1,0:T(8,128)(2,1)S(1)}, bf16[1,1,8,16,512]{4,3,2,1,0:T(8,128)(2,1)S(1)}, u32[]{:S(2)}, u32[]{:S(2)}) %collective-permute-start.7) | collective-permute-done | bytes 131104 | tf_op jit(solution)/shard_map/ppermute | solution.py:12
  19.4 3.6 %collective-permute-start.8 = (bf16[1,1,8,16,512]{4,3,2,1,0:T(8,128)(2,1)S(1)}, bf16[1,1,8,16,512]{4,3,2,1,0:T(8,128)(2,1)S(1)}, u32[]{:S(2)}, u32[]{:S(2)}) collective-permute-start(bf16[1,1,8,16,512]{4,3,2,1,0:T(8,128)(2,1)S(1)} %get-tuple-element.38), channel_id=1, source_target_pairs={{16,0},{32,16},{48,32},{64,48},{80,64},{96,80},{112,96},{128,112},... | collective-permute-start | bytes 393224 | tf_op jit(solution)/shard_map/ppermute | solution.py:12
  23.1 3.5 %collective-permute-done.8 = bf16[1,1,8,16,512]{4,3,2,1,0:T(8,128)(2,1)S(1)} collective-permute-done((bf16[1,1,8,16,512]{4,3,2,1,0:T(8,128)(2,1)S(1)}, bf16[1,1,8,16,512]{4,3,2,1,0:T(8,128)(2,1)S(1)}, u32[]{:S(2)}, u32[]{:S(2)}) %collective-permute-start.8) | collective-permute-done | bytes 131104 | tf_op jit(solution)/shard_map/ppermute | solution.py:12
  28.9 1.6 %collective-permute-done.4 = bf16[3,1,2,8,16,512]{5,4,3,2,1,0:T(8,128)(2,1)S(1)} collective-permute-done((bf16[3,1,2,8,16,512]{5,4,3,2,1,0:T(8,128)(2,1)S(1)}, bf16[3,1,2,8,16,512]{5,4,3,2,1,0:T(8,128)(2,1)S(1)}, u32[]{:S(2)}, u32[]{:S(2)}) %collective-permute-start.4) | collective-permute-done | bytes 786464 | tf_op jit(solution)/shard_map/ppermute | solution.py:89
  36.5 0.8 fusion.67
  37.3 0.8 fusion.73
  38.1 0.8 fusion.79
  39.0 0.8 fusion.57
  40.5 0.8 fusion.51
  41.4 1.2 %collective-permute-start.9 = (f32[108,128]{1,0:T(8,128)S(1)}, f32[108,128]{1,0:T(8,128)S(1)}, u32[]{:S(2)}, u32[]{:S(2)}) collective-permute-start(f32[108,128]{1,0:T(8,128)S(1)} %get-tuple-element.46), channel_id=1, source_target_pairs={{0,17},{1,16},{16,1},{17,0},{32,49},{33,48},{48,33},{49,32},{64,81... | collective-permute-start | bytes 165896 | tf_op jit(solution)/shard_map/ppermute | solution.py:65
  42.5 2.5 %collective-permute-start.10 = (f32[108,128]{1,0:T(8,128)S(1)}, f32[108,128]{1,0:T(8,128)S(1)}, u32[]{:S(2)}, u32[]{:S(2)}) collective-permute-start(f32[108,128]{1,0:T(8,128)S(1)} %get-tuple-element.45), channel_id=1, source_target_pairs={{0,16},{1,17},{16,0},{17,1},{32,48},{33,49},{48,32},{49,33},{64,80... | collective-permute-start | bytes 165896 | tf_op jit(solution)/shard_map/ppermute | solution.py:65
  45.0 2.0 %collective-permute-done.9 = f32[108,128]{1,0:T(8,128)S(1)} collective-permute-done((f32[108,128]{1,0:T(8,128)S(1)}, f32[108,128]{1,0:T(8,128)S(1)}, u32[]{:S(2)}, u32[]{:S(2)}) %collective-permute-start.9) | collective-permute-done | bytes 55328 | tf_op jit(solution)/shard_map/ppermute | solution.py:65
  47.0 1.1 %collective-permute-done.10 = f32[108,128]{1,0:T(8,128)S(1)} collective-permute-done((f32[108,128]{1,0:T(8,128)S(1)}, f32[108,128]{1,0:T(8,128)S(1)}, u32[]{:S(2)}, u32[]{:S(2)}) %collective-permute-start.10) | collective-permute-done | bytes 55328 | tf_op jit(solution)/shard_map/ppermute | solution.py:65
  48.2 1.0 %collective-permute-done.11 = f32[108,128]{1,0:T(8,128)S(1)} collective-permute-done((f32[108,128]{1,0:T(8,128)S(1)}, f32[108,128]{1,0:T(8,128)S(1)}, u32[]{:S(2)}, u32[]{:S(2)}) %collective-permute-start.11) | collective-permute-done | bytes 55328 | tf_op jit(solution)/shard_map/ppermute | solution.py:65
  49.2 0.8 %collective-permute-start.12 = (f32[108,128]{1,0:T(8,128)S(1)}, f32[108,128]{1,0:T(8,128)S(1)}, u32[]{:S(2)}, u32[]{:S(2)}) collective-permute-start(f32[108,128]{1,0:T(8,128)S(1)} %fusion.100), channel_id=1, source_target_pairs={{0,160},{1,161},{16,176},{17,177},{32,128},{33,129},{48,144},{49,1... | collective-permute-start | bytes 165896 | tf_op jit(solution)/shard_map/ppermute | solution.py:26
  50.1 2.7 %collective-permute-start.13 = (f32[108,128]{1,0:T(8,128)S(1)}, f32[108,128]{1,0:T(8,128)S(1)}, u32[]{:S(2)}, u32[]{:S(2)}) collective-permute-start(f32[108,128]{1,0:T(8,128)S(1)} %fusion.100), channel_id=1, source_target_pairs={{0,128},{1,129},{16,144},{17,145},{32,160},{33,161},{48,176},{49,1... | collective-permute-start | bytes 165896 | tf_op jit(solution)/shard_map/ppermute | solution.py:26
  52.8 2.4 %collective-permute-start.14 = (f32[108,128]{1,0:T(8,128)S(1)}, f32[108,128]{1,0:T(8,128)S(1)}, u32[]{:S(2)}, u32[]{:S(2)}) collective-permute-start(f32[108,128]{1,0:T(8,128)S(1)} %fusion.100), channel_id=1, source_target_pairs={{0,32},{1,33},{16,48},{17,49},{32,0},{33,1},{48,16},{49,17},{64,96... | collective-permute-start | bytes 165896 | tf_op jit(solution)/shard_map/ppermute | solution.py:26
  55.2 2.3 %collective-permute-done.12 = f32[108,128]{1,0:T(8,128)S(1)} collective-permute-done((f32[108,128]{1,0:T(8,128)S(1)}, f32[108,128]{1,0:T(8,128)S(1)}, u32[]{:S(2)}, u32[]{:S(2)}) %collective-permute-start.12) | collective-permute-done | bytes 55328 | tf_op jit(solution)/shard_map/ppermute | solution.py:26
  57.9 3.5 %collective-permute-start.15 = (f32[108,128]{1,0:T(8,128)S(1)}, f32[108,128]{1,0:T(8,128)S(1)}, u32[]{:S(2)}, u32[]{:S(2)}) collective-permute-start(f32[108,128]{1,0:T(8,128)S(1)} %add_add_fusion), channel_id=1, source_target_pairs={{0,64},{1,65},{16,80},{17,81},{32,96},{33,97},{48,112},{49,113},{6... | collective-permute-start | bytes 165896 | tf_op jit(solution)/shard_map/ppermute | solution.py:26
  61.4 4.5 %collective-permute-start.5 = (f32[1,1,8,16,512]{4,3,2,1,0:T(8,128)S(1)}, f32[1,1,8,16,512]{4,3,2,1,0:T(8,128)S(1)}, u32[]{:S(2)}, u32[]{:S(2)}) collective-permute-start(f32[1,1,8,16,512]{4,3,2,1,0:T(8,128)S(1)} %get-tuple-element.36), channel_id=1, source_target_pairs={{0,16},{16,32},{32,48},{48,64},{64,80},{80,96},{96,112},{112,128},... | collective-permute-start | bytes 786440 | tf_op jit(solution)/shard_map/ppermute | solution.py:12
  66.0 1.1 %collective-permute-done.15 = f32[108,128]{1,0:T(8,128)S(1)} collective-permute-done((f32[108,128]{1,0:T(8,128)S(1)}, f32[108,128]{1,0:T(8,128)S(1)}, u32[]{:S(2)}, u32[]{:S(2)}) %collective-permute-start.15) | collective-permute-done | bytes 55328 | tf_op jit(solution)/shard_map/ppermute | solution.py:26
  67.1 1.9 %collective-permute-start.16 = (f32[108,128]{1,0:T(8,128)S(1)}, f32[108,128]{1,0:T(8,128)S(1)}, u32[]{:S(2)}, u32[]{:S(2)}) collective-permute-start(f32[108,128]{1,0:T(8,128)S(1)} %select_add_fusion), channel_id=1, source_target_pairs={{0,17},{1,16},{16,1},{17,0},{32,49},{33,48},{48,33},{49,32},{64,81... | collective-permute-start | bytes 165896 | tf_op jit(solution)/shard_map/ppermute | solution.py:74
  69.3 1.4 %collective-permute-start.18 = (f32[108,128]{1,0:T(8,128)S(1)}, f32[108,128]{1,0:T(8,128)S(1)}, u32[]{:S(2)}, u32[]{:S(2)}) collective-permute-start(f32[108,128]{1,0:T(8,128)S(1)} %select_add_fusion), channel_id=1, source_target_pairs={{0,1},{1,0},{16,17},{17,16},{32,33},{33,32},{48,49},{49,48},{64,65... | collective-permute-start | bytes 165896 | tf_op jit(solution)/shard_map/ppermute | solution.py:74
  70.7 6.4 %collective-permute-start.6 = (f32[1,1,8,16,512]{4,3,2,1,0:T(8,128)S(1)}, f32[1,1,8,16,512]{4,3,2,1,0:T(8,128)S(1)}, u32[]{:S(2)}, u32[]{:S(2)}) collective-permute-start(f32[1,1,8,16,512]{4,3,2,1,0:T(8,128)S(1)} %get-tuple-element.35), channel_id=1, source_target_pairs={{16,0},{32,16},{48,32},{64,48},{80,64},{96,80},{112,96},{128,112},... | collective-permute-start | bytes 786440 | tf_op jit(solution)/shard_map/ppermute | solution.py:12
  77.8 3.1 %collective-permute-done.6 = f32[1,1,8,16,512]{4,3,2,1,0:T(8,128)S(1)} collective-permute-done((f32[1,1,8,16,512]{4,3,2,1,0:T(8,128)S(1)}, f32[1,1,8,16,512]{4,3,2,1,0:T(8,128)S(1)}, u32[]{:S(2)}, u32[]{:S(2)}) %collective-permute-start.6) | collective-permute-done | bytes 262176 | tf_op jit(solution)/shard_map/ppermute | solution.py:12
  80.9 0.8 fusion.93
  (68 shorter events, 10.8 us)
Async XLA Ops:
  0.6 12.0 %copy-start.1 = (bf16[1,2,8,16,512]{4,3,2,1,0:T(8,128)(2,1)S(1)}, bf16[1,2,8,16,512]{4,3,2,1,0:T(8,128)(2,1)}, u32[]{:S(2)}) copy-start(bf16[1,2,8,16,512]{4,3,2,1,0:T(8,128)(2,1)} %param.4) | copy-start | bytes 786436
  0.6 22.4 %copy-start = (bf16[1,2,8,16,512]{4,3,2,1,0:T(8,128)(2,1)S(1)}, bf16[1,2,8,16,512]{4,3,2,1,0:T(8,128)(2,1)}, u32[]{:S(2)}) copy-start(bf16[1,2,8,16,512]{4,3,2,1,0:T(8,128)(2,1)} %param.3) | copy-start | bytes 786436
  0.6 27.2 %collective-permute-start = (bf16[1,2,8,16,512]{4,3,2,1,0:T(8,128)(2,1)}, bf16[1,2,8,16,512]{4,3,2,1,0:T(8,128)(2,1)S(1)}, u32[]{:S(2)}, u32[]{:S(2)}) collective-permute-start(bf16[1,2,8,16,512]{4,3,2,1,0:T(8,128)(2,1)} %param.4), channel_id=1, source_target_pairs={{0,4},{2,6},{4,8},{6,10},{8,12},{10,14},{12,0},{14,2},{1,5},{3,7},... | collective-permute-start | bytes 786440 | tf_op jit(solution)/shard_map/ppermute | solution.py:84
  2.3 25.6 %collective-permute-start.1 = (bf16[1,2,8,16,512]{4,3,2,1,0:T(8,128)(2,1)}, bf16[1,2,8,16,512]{4,3,2,1,0:T(8,128)(2,1)S(1)}, u32[]{:S(2)}, u32[]{:S(2)}) collective-permute-start(bf16[1,2,8,16,512]{4,3,2,1,0:T(8,128)(2,1)} %param.4), channel_id=1, source_target_pairs={{0,8},{2,10},{4,12},{6,14},{8,0},{10,2},{12,4},{14,6},{1,9},{3,11}... | collective-permute-start | bytes 786440 | tf_op jit(solution)/shard_map/ppermute | solution.py:84
  5.2 22.7 %collective-permute-start.2 = (bf16[1,2,8,16,512]{4,3,2,1,0:T(8,128)(2,1)}, bf16[1,2,8,16,512]{4,3,2,1,0:T(8,128)(2,1)S(1)}, u32[]{:S(2)}, u32[]{:S(2)}) collective-permute-start(bf16[1,2,8,16,512]{4,3,2,1,0:T(8,128)(2,1)} %param.4), channel_id=1, source_target_pairs={{0,12},{2,14},{4,0},{6,2},{8,4},{10,6},{12,8},{14,10},{1,13},{3,15... | collective-permute-start | bytes 786440 | tf_op jit(solution)/shard_map/ppermute | solution.py:84
  6.6 22.3 %collective-permute-start.3 = (bf16[1,2,8,16,512]{4,3,2,1,0:T(8,128)(2,1)}, bf16[1,2,8,16,512]{4,3,2,1,0:T(8,128)(2,1)S(1)}, u32[]{:S(2)}, u32[]{:S(2)}) collective-permute-start(bf16[1,2,8,16,512]{4,3,2,1,0:T(8,128)(2,1)} %param.4), channel_id=1, source_target_pairs={{0,2},{2,0},{4,6},{6,4},{8,10},{10,8},{12,14},{14,12},{1,3},{3,1},... | collective-permute-start | bytes 786440 | tf_op jit(solution)/shard_map/ppermute | solution.py:89
  7.5 11.9 %collective-permute-start.7 = (bf16[1,1,8,16,512]{4,3,2,1,0:T(8,128)(2,1)S(1)}, bf16[1,1,8,16,512]{4,3,2,1,0:T(8,128)(2,1)S(1)}, u32[]{:S(2)}, u32[]{:S(2)}) collective-permute-start(bf16[1,1,8,16,512]{4,3,2,1,0:T(8,128)(2,1)S(1)} %get-tuple-element.39), channel_id=1, source_target_pairs={{0,16},{16,32},{32,48},{48,64},{64,80},{80,96},{96,112},{112,128},... | collective-permute-start | bytes 393224 | tf_op jit(solution)/shard_map/ppermute | solution.py:12
  19.4 7.2 %collective-permute-start.8 = (bf16[1,1,8,16,512]{4,3,2,1,0:T(8,128)(2,1)S(1)}, bf16[1,1,8,16,512]{4,3,2,1,0:T(8,128)(2,1)S(1)}, u32[]{:S(2)}, u32[]{:S(2)}) collective-permute-start(bf16[1,1,8,16,512]{4,3,2,1,0:T(8,128)(2,1)S(1)} %get-tuple-element.38), channel_id=1, source_target_pairs={{16,0},{32,16},{48,32},{64,48},{80,64},{96,80},{112,96},{128,112},... | collective-permute-start | bytes 393224 | tf_op jit(solution)/shard_map/ppermute | solution.py:12
  28.0 2.6 %collective-permute-start.4 = (bf16[3,1,2,8,16,512]{5,4,3,2,1,0:T(8,128)(2,1)S(1)}, bf16[3,1,2,8,16,512]{5,4,3,2,1,0:T(8,128)(2,1)S(1)}, u32[]{:S(2)}, u32[]{:S(2)}) collective-permute-start(bf16[3,1,2,8,16,512]{5,4,3,2,1,0:T(8,128)(2,1)S(1)} %pad_maximum_fusion), channel_id=1, source_target_pairs={{0,2},{2,0},{4,6},{6,4},{8,10},{10,8},{12,14},{14,12},{1,3},{3,1},... | collective-permute-start | bytes 2359304 | tf_op jit(solution)/shard_map/ppermute | solution.py:89
  41.4 5.7 %collective-permute-start.9 = (f32[108,128]{1,0:T(8,128)S(1)}, f32[108,128]{1,0:T(8,128)S(1)}, u32[]{:S(2)}, u32[]{:S(2)}) collective-permute-start(f32[108,128]{1,0:T(8,128)S(1)} %get-tuple-element.46), channel_id=1, source_target_pairs={{0,17},{1,16},{16,1},{17,0},{32,49},{33,48},{48,33},{49,32},{64,81... | collective-permute-start | bytes 165896 | tf_op jit(solution)/shard_map/ppermute | solution.py:65
  42.5 5.7 %collective-permute-start.10 = (f32[108,128]{1,0:T(8,128)S(1)}, f32[108,128]{1,0:T(8,128)S(1)}, u32[]{:S(2)}, u32[]{:S(2)}) collective-permute-start(f32[108,128]{1,0:T(8,128)S(1)} %get-tuple-element.45), channel_id=1, source_target_pairs={{0,16},{1,17},{16,0},{17,1},{32,48},{33,49},{48,32},{49,33},{64,80... | collective-permute-start | bytes 165896 | tf_op jit(solution)/shard_map/ppermute | solution.py:65
  45.0 4.2 %collective-permute-start.11 = (f32[108,128]{1,0:T(8,128)S(1)}, f32[108,128]{1,0:T(8,128)S(1)}, u32[]{:S(2)}, u32[]{:S(2)}) collective-permute-start(f32[108,128]{1,0:T(8,128)S(1)} %get-tuple-element.44), channel_id=1, source_target_pairs={{0,1},{1,0},{16,17},{17,16},{32,33},{33,32},{48,49},{49,48},{64,65... | collective-permute-start | bytes 165896 | tf_op jit(solution)/shard_map/ppermute | solution.py:65
  49.2 8.2 %collective-permute-start.12 = (f32[108,128]{1,0:T(8,128)S(1)}, f32[108,128]{1,0:T(8,128)S(1)}, u32[]{:S(2)}, u32[]{:S(2)}) collective-permute-start(f32[108,128]{1,0:T(8,128)S(1)} %fusion.100), channel_id=1, source_target_pairs={{0,160},{1,161},{16,176},{17,177},{32,128},{33,129},{48,144},{49,1... | collective-permute-start | bytes 165896 | tf_op jit(solution)/shard_map/ppermute | solution.py:26
  50.1 7.4 %collective-permute-start.13 = (f32[108,128]{1,0:T(8,128)S(1)}, f32[108,128]{1,0:T(8,128)S(1)}, u32[]{:S(2)}, u32[]{:S(2)}) collective-permute-start(f32[108,128]{1,0:T(8,128)S(1)} %fusion.100), channel_id=1, source_target_pairs={{0,128},{1,129},{16,144},{17,145},{32,160},{33,161},{48,176},{49,1... | collective-permute-start | bytes 165896 | tf_op jit(solution)/shard_map/ppermute | solution.py:26
  52.8 5.1 %collective-permute-start.14 = (f32[108,128]{1,0:T(8,128)S(1)}, f32[108,128]{1,0:T(8,128)S(1)}, u32[]{:S(2)}, u32[]{:S(2)}) collective-permute-start(f32[108,128]{1,0:T(8,128)S(1)} %fusion.100), channel_id=1, source_target_pairs={{0,32},{1,33},{16,48},{17,49},{32,0},{33,1},{48,16},{49,17},{64,96... | collective-permute-start | bytes 165896 | tf_op jit(solution)/shard_map/ppermute | solution.py:26
  57.9 9.1 %collective-permute-start.15 = (f32[108,128]{1,0:T(8,128)S(1)}, f32[108,128]{1,0:T(8,128)S(1)}, u32[]{:S(2)}, u32[]{:S(2)}) collective-permute-start(f32[108,128]{1,0:T(8,128)S(1)} %add_add_fusion), channel_id=1, source_target_pairs={{0,64},{1,65},{16,80},{17,81},{32,96},{33,97},{48,112},{49,113},{6... | collective-permute-start | bytes 165896 | tf_op jit(solution)/shard_map/ppermute | solution.py:26
  61.4 16.4 %collective-permute-start.5 = (f32[1,1,8,16,512]{4,3,2,1,0:T(8,128)S(1)}, f32[1,1,8,16,512]{4,3,2,1,0:T(8,128)S(1)}, u32[]{:S(2)}, u32[]{:S(2)}) collective-permute-start(f32[1,1,8,16,512]{4,3,2,1,0:T(8,128)S(1)} %get-tuple-element.36), channel_id=1, source_target_pairs={{0,16},{16,32},{32,48},{48,64},{64,80},{80,96},{96,112},{112,128},... | collective-permute-start | bytes 786440 | tf_op jit(solution)/shard_map/ppermute | solution.py:12
  67.1 10.0 %collective-permute-start.16 = (f32[108,128]{1,0:T(8,128)S(1)}, f32[108,128]{1,0:T(8,128)S(1)}, u32[]{:S(2)}, u32[]{:S(2)}) collective-permute-start(f32[108,128]{1,0:T(8,128)S(1)} %select_add_fusion), channel_id=1, source_target_pairs={{0,17},{1,16},{16,1},{17,0},{32,49},{33,48},{48,33},{49,32},{64,81... | collective-permute-start | bytes 165896 | tf_op jit(solution)/shard_map/ppermute | solution.py:74
  68.9 8.2 %collective-permute-start.17 = (f32[108,128]{1,0:T(8,128)S(1)}, f32[108,128]{1,0:T(8,128)S(1)}, u32[]{:S(2)}, u32[]{:S(2)}) collective-permute-start(f32[108,128]{1,0:T(8,128)S(1)} %select_add_fusion), channel_id=1, source_target_pairs={{0,16},{1,17},{16,0},{17,1},{32,48},{33,49},{48,32},{49,33},{64,80... | collective-permute-start | bytes 165896 | tf_op jit(solution)/shard_map/ppermute | solution.py:74
  69.3 7.8 %collective-permute-start.18 = (f32[108,128]{1,0:T(8,128)S(1)}, f32[108,128]{1,0:T(8,128)S(1)}, u32[]{:S(2)}, u32[]{:S(2)}) collective-permute-start(f32[108,128]{1,0:T(8,128)S(1)} %select_add_fusion), channel_id=1, source_target_pairs={{0,1},{1,0},{16,17},{17,16},{32,33},{33,32},{48,49},{49,48},{64,65... | collective-permute-start | bytes 165896 | tf_op jit(solution)/shard_map/ppermute | solution.py:74
  70.7 10.2 %collective-permute-start.6 = (f32[1,1,8,16,512]{4,3,2,1,0:T(8,128)S(1)}, f32[1,1,8,16,512]{4,3,2,1,0:T(8,128)S(1)}, u32[]{:S(2)}, u32[]{:S(2)}) collective-permute-start(f32[1,1,8,16,512]{4,3,2,1,0:T(8,128)S(1)} %get-tuple-element.35), channel_id=1, source_target_pairs={{16,0},{32,16},{48,32},{64,48},{80,64},{96,80},{112,96},{128,112},... | collective-permute-start | bytes 786440 | tf_op jit(solution)/shard_map/ppermute | solution.py:12
